TPU v7x, 512 devices: a whole 4x8x8 slice. The times are simulated.
512 devices in a mesh: dp: 4 (over x), seq: 16 (over z, core), head: 8 (over y).
Axes of the slice: x: 4, y: 8, z: 8, core: 2. Of those that a mesh axis runs over, the one named last changes fastest.
Arguments:
- doc_ids: int32 [16384], P(('dp', 'seq')), parts along dimension 0, may hold values from 0 to 7, never falling along the last dimension, each value on 1 to 2048 neighbouring positions
- light_q: bfloat16 [16384, 4096], P(('dp', 'seq'), 'head'), parts along dimension 0, may hold values from -0.59765625 to 0.59765625
- light_k: bfloat16 [16384, 4096], P(('dp', 'seq'), 'head'), parts along dimension 0, may hold values from -0.59765625 to 0.59765625
- light_v: bfloat16 [16384, 4096], P(('dp', 'seq'), 'head'), parts along dimension 0, may hold values from -6 to 6
- light_decay: float32 [32], P('head'), may hold values from 0 to 1
- light_grad_out: bfloat16 [16384, 4096], P(('dp', 'seq'), 'head'), parts along dimension 0, may hold values from -6 to 6
- soft_q: bfloat16 [16384, 4096], P(('dp', 'seq'), 'head'), parts along dimension 0, may hold values from -40 to 40
- soft_k: bfloat16 [16384, 4096], P(('dp', 'seq'), 'head'), parts along dimension 0, may hold values from -40 to 40
- soft_v: bfloat16 [16384, 4096], P(('dp', 'seq'), 'head'), parts along dimension 0, may hold values from -6 to 6
- soft_grad_out: bfloat16 [16384, 4096], P(('dp', 'seq'), 'head'), parts along dimension 0, may hold values from -6 to 6
Outputs:
- lightning_output: bfloat16 [16384, 4096], P(('dp', 'seq'), 'head'), parts along dimension 0
- lightning_query_gradient: bfloat16 [16384, 4096], P(('dp', 'seq'), 'head'), parts along dimension 0
- lightning_key_gradient: bfloat16 [16384, 4096], P(('dp', 'seq'), 'head'), parts along dimension 0
- lightning_value_gradient: bfloat16 [16384, 4096], P(('dp', 'seq'), 'head'), parts along dimension 0
- soft_out: bfloat16 [16384, 4096], P(('dp', 'seq'), 'head'), parts along dimension 0
- soft_dq: bfloat16 [16384, 4096], P(('dp', 'seq'), 'head'), parts along dimension 0
- soft_dk: bfloat16 [16384, 4096], P(('dp', 'seq'), 'head'), parts along dimension 0
- soft_dv: bfloat16 [16384, 4096], P(('dp', 'seq'), 'head'), parts along dimension 0
There are 4 independent parts, one for each index of `dp`. A program takes and returns all parts, laid end to end along the dimension named above; an argument that names none is the same for every part. Nothing has to cross between parts.
Inputs may be any that keep to these rules, and one draw needn't show every extreme that they name: `doc_ids`: document ids never fall along the sequence; each document holds at most 2048 tokens, and one holds exactly that many.
All inputs are finite; a program needn't handle non-finite values.
Results may differ from a plain program's by a relative error of at most 0.02.
Values may be sent and summed in bfloat16 or wider, within the bound.
No kernel may reach another device: no remote copies, remote signals or barrier semaphores. Data moves between devices by JAX's collectives and lax.ppermute only.
A program may use at most 128 MiB of HBM per device.

v0:
```python
import jax
import jax.numpy as jnp
from jax import lax
from jax.sharding import PartitionSpec as P

PRECISE = lax.Precision.HIGH


def entering(part, axis, combine, identity, reverse):
    count = lax.axis_size(axis)
    place = lax.axis_index(axis)
    ahead = count - 1 - place if reverse else place
    gathered = jax.tree.map(lambda a: lax.all_gather(a, axis), part)
    state = jax.tree.map(lambda a, e: jnp.zeros_like(a) + jnp.asarray(e, a.dtype), part, identity)

    def one(lap, state):
        source = count - 1 - lap if reverse else lap
        return combine(
            state, jax.tree.map(lambda a: lax.dynamic_index_in_dim(a, source, 0, False), gathered)
        )

    return lax.fori_loop(0, ahead, one, state)


def from_behind(value, axis, steps):
    count = lax.axis_size(axis)
    first, last = (max(0, -steps), min(count, count - steps))
    return lax.ppermute(value, axis, [(source, source + steps) for source in range(first, last)])


def join_forward(earlier, later):
    state_a, keep_a, head_a, tail_a = earlier
    state_b, keep_b, head_b, tail_b = later
    empty_a = tail_a < 0
    empty_b = tail_b < 0
    joined = (head_b == tail_b) & (head_b == tail_a)
    running_state = jnp.where(
        empty_b, state_a, jnp.where(joined, keep_b[:, None, None] * state_a + state_b, state_b)
    )
    return (
        running_state,
        keep_a * keep_b,
        jnp.where(empty_a, head_b, head_a),
        jnp.where(empty_b, tail_a, tail_b),
    )


def join_backward(earlier, later):
    state_h, keep_h, head_h, tail_h = earlier
    state_l, keep_l, head_l, tail_l = later
    empty_h = tail_h < 0
    empty_l = tail_l < 0
    joined = (head_l == tail_l) & (tail_l == head_h)
    running_state = jnp.where(
        empty_l, state_h, jnp.where(joined, keep_l[:, None, None] * state_h + state_l, state_l)
    )
    return (
        running_state,
        keep_h * keep_l,
        jnp.where(empty_l, head_h, head_l),
        jnp.where(empty_h, tail_l, tail_h),
    )


def mixed_result(form, left, right):
    return jnp.einsum(form, left, right, precision=PRECISE, preferred_element_type=jnp.float32)


def per_device(
    doc_ids,
    light_q,
    light_k,
    light_v,
    light_decay,
    light_grad_out,
    soft_q,
    soft_k,
    soft_v,
    soft_grad_out,
):
    tok_rows = light_q.shape[0]
    heads = light_decay.shape[0]
    width = light_q.shape[1] // heads
    shards = lax.axis_size("seq")
    total_rows = tok_rows * shards
    offset = lax.axis_index("seq") * tok_rows
    last_pos = offset + tok_rows - 1
    all_ids = lax.all_gather(doc_ids, "seq", axis=0, tiled=True)
    positions = offset + jnp.arange(tok_rows, dtype=jnp.int32)
    own_ids = doc_ids.astype(jnp.float32)
    within_segment_position = jnp.arange(tok_rows, dtype=jnp.int32)
    reach = min(shards - 1, (tok_rows + total_rows // 2 - 2) // tok_rows)
    query_half_rows = light_q.reshape(tok_rows, heads, width)
    key_half_rows = light_k.reshape(tok_rows, heads, width)
    value_half_rows = light_v.reshape(tok_rows, heads, width)
    backward_sequence_share = light_grad_out.reshape(tok_rows, heads, width)
    inside = (doc_ids[:, None] == doc_ids[None, :]) & (
        within_segment_position[None, :] <= within_segment_position[:, None]
    )
    distance = jnp.maximum(
        within_segment_position[:, None] - within_segment_position[None, :], 0
    ).astype(jnp.float32)
    weight = jnp.where(inside[None], jnp.exp(-light_decay[:, None, None] * distance[None]), 0.0)
    scores = (
        jnp.einsum(
            "thd,shd->hts", query_half_rows, key_half_rows, preferred_element_type=jnp.float32
        )
        * weight
    )
    lightning_output = mixed_result("hts,shd->thd", scores, value_half_rows)
    head_id = own_ids[0]
    tail_id = own_ids[-1]
    since_start = (within_segment_position + 1).astype(jnp.float32)
    until_end = (tok_rows - 1 - within_segment_position).astype(jnp.float32)
    start_decay = jnp.exp(-since_start[:, None] * light_decay[None, :])
    end_decay = jnp.exp(-until_end[:, None] * light_decay[None, :])
    offset_to_end = end_decay * (own_ids == tail_id)[:, None]
    running_state = mixed_result(
        "bto,btq->toq", key_half_rows * offset_to_end[:, :, None], value_half_rows
    )
    keep = jnp.exp(-light_decay * tok_rows)
    identity = (
        jnp.zeros_like(running_state),
        jnp.ones_like(keep),
        jnp.float32(-1.0),
        jnp.float32(-1.0),
    )
    inherited_memory_matrix, _, _, carried_id = entering(
        (running_state, keep, head_id, tail_id), "seq", join_forward, identity, False
    )
    distance_since_beginning = start_decay * (own_ids == carried_id)[:, None]
    lightning_output = lightning_output + mixed_result(
        "peb,ebi->pei",
        query_half_rows * distance_since_beginning[:, :, None],
        inherited_memory_matrix,
    )
    grad_scores = (
        jnp.einsum(
            "thv,shv->hts",
            backward_sequence_share,
            value_half_rows,
            preferred_element_type=jnp.float32,
        )
        * weight
    )
    lightning_query_gradient = mixed_result("hts,shk->thk", grad_scores, key_half_rows)
    lightning_query_gradient = lightning_query_gradient + mixed_result(
        "mcq,cxq->mcx",
        backward_sequence_share * distance_since_beginning[:, :, None],
        inherited_memory_matrix,
    )
    lightning_key_gradient = mixed_result("hts,thk->shk", grad_scores, query_half_rows)
    lightning_value_gradient = mixed_result("hts,thv->shv", scores, backward_sequence_share)
    opening_part = start_decay * (own_ids == head_id)[:, None]
    pending_state = mixed_result(
        "ejn,ejf->jnf", query_half_rows * opening_part[:, :, None], backward_sequence_share
    )
    returned_value, _, yielded_document_number, _ = entering(
        (pending_state, keep, head_id, tail_id), "seq", join_backward, identity, True
    )
    closing_part = (end_decay * (own_ids == yielded_document_number)[:, None])[:, :, None]
    lightning_key_gradient = (
        lightning_key_gradient
        + mixed_result("qpb,aqb->aqp", returned_value, value_half_rows) * closing_part
    )
    lightning_value_gradient = (
        lightning_value_gradient
        + mixed_result("dgp,zdg->zdp", returned_value, key_half_rows) * closing_part
    )
    scale = width ** (-0.5)
    soft_query = soft_q.reshape(tok_rows, heads, width)
    soft_grads = soft_grad_out.reshape(tok_rows, heads, width)
    soft_keys = soft_k.reshape(tok_rows, heads, width)
    soft_values = soft_v.reshape(tok_rows, heads, width)
    all_keys, all_values = (
        lax.all_gather(soft_k, "seq", axis=0, tiled=True),
        lax.all_gather(soft_v, "seq", axis=0, tiled=True),
    )
    first_pos = jnp.sum(all_ids < doc_ids[0])
    doc_end = jnp.sum(all_ids <= doc_ids[-1]) - 1
    key_block = min(512, total_rows)
    key_count = total_rows // key_block
    block_order = jnp.arange(key_count, dtype=jnp.int32)

    def key_mask(start, count):
        key_pos = start + jnp.arange(count, dtype=jnp.int32)
        key_ids = lax.dynamic_slice_in_dim(all_ids, start, count)
        return (key_pos[None, :] <= positions[:, None]) & (key_ids[None, :] == doc_ids[:, None])

    def held_block(start):
        segment_attention_inputs = lax.dynamic_slice_in_dim(all_keys, start, key_block).reshape(
            key_block, heads, width
        )
        block_values = lax.dynamic_slice_in_dim(all_values, start, key_block).reshape(
            key_block, heads, width
        )
        return (segment_attention_inputs, block_values)

    def unused(start):
        return (start > last_pos) | (start + key_block - 1 < first_pos)

    def forward_block(carry, index):
        start = index * key_block

        def forward_update(inner):
            top, total, accum = inner
            segment_attention_inputs, block_values = held_block(start)
            allowed = key_mask(start, key_block)[None]
            logits = (
                jnp.einsum(
                    "thd,shd->hts",
                    soft_query,
                    segment_attention_inputs,
                    preferred_element_type=jnp.float32,
                )
                * scale
            )
            logits = jnp.where(allowed, logits, -1e30)
            fresh = jnp.maximum(top, jnp.max(logits, axis=2))
            factor = jnp.exp(top - fresh)
            expo = jnp.where(allowed, jnp.exp(logits - fresh[:, :, None]), 0.0)
            total = total * factor + jnp.sum(expo, axis=2)
            accum = accum * factor[:, :, None] + jnp.einsum(
                "hts,shd->htd",
                expo.astype(jnp.bfloat16),
                block_values,
                preferred_element_type=jnp.float32,
            )
            return (fresh, total, accum)

        return (lax.cond(unused(start), lambda inner: inner, forward_update, carry), None)

    start_carry = (
        jnp.full((heads, tok_rows), -1e30, jnp.float32),
        jnp.zeros((heads, tok_rows), jnp.float32),
        jnp.zeros((heads, tok_rows, width), jnp.float32),
    )
    (top, total, accum), _ = lax.scan(forward_block, start_carry, block_order)
    soft_out = jnp.transpose(accum / total[:, :, None], (1, 0, 2)).astype(jnp.bfloat16)
    lse = top + jnp.log(total)
    delta = jnp.sum(soft_grads.astype(jnp.float32) * soft_out.astype(jnp.float32), axis=2).T
    all_lse, all_delta = (
        lax.all_gather(lse, "seq", axis=1, tiled=True),
        lax.all_gather(delta, "seq", axis=1, tiled=True),
    )
    zero_rows = jnp.zeros((tok_rows, heads, width), jnp.float32)

    def query_block(carry, index):
        start = index * key_block

        def query_update(inner):
            segment_attention_inputs, block_values = held_block(start)
            allowed = key_mask(start, key_block)[None]
            logits = (
                jnp.einsum(
                    "thd,shd->hts",
                    soft_query,
                    segment_attention_inputs,
                    preferred_element_type=jnp.float32,
                )
                * scale
            )
            prob = jnp.where(
                allowed, jnp.exp(jnp.where(allowed, logits - lse[:, :, None], -1e30)), 0.0
            )
            dprob = jnp.einsum(
                "thd,shd->hts", soft_grads, block_values, preferred_element_type=jnp.float32
            )
            dlogit = (prob * (dprob - delta[:, :, None])).astype(jnp.bfloat16)
            return (
                inner
                + jnp.einsum(
                    "hts,shd->thd",
                    dlogit,
                    segment_attention_inputs,
                    preferred_element_type=jnp.float32,
                )
                * scale
            )

        return (lax.cond(unused(start), lambda inner: inner, query_update, carry), None)

    soft_dq, _ = lax.scan(query_block, zero_rows, block_order)

    def key_terms(piece_query, piece_grads, start, count):
        query_pos = start + jnp.arange(count, dtype=jnp.int32)
        query_ids = lax.dynamic_slice_in_dim(all_ids, start, count)
        lse_part = lax.dynamic_slice_in_dim(all_lse, start, count, 1)
        delta_part = lax.dynamic_slice_in_dim(all_delta, start, count, 1)
        allowed = (
            (positions[None, :] <= query_pos[:, None]) & (doc_ids[None, :] == query_ids[:, None])
        )[None]
        logits = (
            jnp.einsum("thd,shd->hts", piece_query, soft_keys, preferred_element_type=jnp.float32)
            * scale
        )
        prob = jnp.where(
            allowed, jnp.exp(jnp.where(allowed, logits - lse_part[:, :, None], -1e30)), 0.0
        )
        dv_part = jnp.einsum(
            "hts,thd->shd",
            prob.astype(jnp.bfloat16),
            piece_grads,
            preferred_element_type=jnp.float32,
        )
        dprob = jnp.einsum(
            "thd,shd->hts", piece_grads, soft_values, preferred_element_type=jnp.float32
        )
        dlogit = (prob * (dprob - delta_part[:, :, None])).astype(jnp.bfloat16)
        dk_part = (
            jnp.einsum("hts,thd->shd", dlogit, piece_query, preferred_element_type=jnp.float32)
            * scale
        )
        return (dk_part, dv_part)

    def key_piece(carry, piece_query, piece_grads, start):
        count = piece_query.shape[0]
        span_rows = count
        span_count = count // span_rows

        def span_step(inner, index):
            begin = index * span_rows
            query_part = piece_query.reshape(span_rows, heads, width)
            grads_part = piece_grads.reshape(span_rows, heads, width)
            query_start = start + begin

            def span_update(sums):
                dk_part, dv_part = key_terms(query_part, grads_part, query_start, span_rows)
                return (sums[0] + dk_part, sums[1] + dv_part)

            skipped = (query_start + span_rows - 1 < offset) | (query_start > doc_end)
            return (lax.cond(skipped, lambda sums: sums, span_update, inner), None)

        result, _ = lax.scan(span_step, carry, jnp.arange(span_count, dtype=jnp.int32))
        return result

    grad_pair = key_piece((zero_rows, zero_rows), soft_q, soft_grad_out, offset)
    for step in range(1, reach + 1):
        near_query, near_grads = from_behind((soft_q, soft_grad_out), "seq", -step)
        later_start = jnp.minimum(offset + step * tok_rows, total_rows - tok_rows)
        grad_pair = key_piece(grad_pair, near_query, near_grads, later_start)
    soft_dk, soft_dv = grad_pair
    flat = (tok_rows, heads * width)
    return (
        lightning_output.reshape(flat).astype(jnp.bfloat16),
        lightning_query_gradient.reshape(flat).astype(jnp.bfloat16),
        lightning_key_gradient.reshape(flat).astype(jnp.bfloat16),
        lightning_value_gradient.reshape(flat).astype(jnp.bfloat16),
        soft_out.reshape(flat),
        soft_dq.reshape(flat).astype(jnp.bfloat16),
        soft_dk.reshape(flat).astype(jnp.bfloat16),
        soft_dv.reshape(flat).astype(jnp.bfloat16),
    )


def solution(mesh):
    return jax.shard_map(
        per_device,
        mesh=mesh,
        in_specs=(
            P(("dp", "seq")),
            P(("dp", "seq"), "head"),
            P(("dp", "seq"), "head"),
            P(("dp", "seq"), "head"),
            P("head"),
            P(("dp", "seq"), "head"),
            P(("dp", "seq"), "head"),
            P(("dp", "seq"), "head"),
            P(("dp", "seq"), "head"),
            P(("dp", "seq"), "head"),
        ),
        out_specs=(
            P(("dp", "seq"), "head"),
            P(("dp", "seq"), "head"),
            P(("dp", "seq"), "head"),
            P(("dp", "seq"), "head"),
            P(("dp", "seq"), "head"),
            P(("dp", "seq"), "head"),
            P(("dp", "seq"), "head"),
            P(("dp", "seq"), "head"),
        ),
        check_vma=False,
    )
```

profile of v0, /device:TPU:449, one launch (start us, length us, event | category | flops | bytes accessed | tf_op | source)
XLA Modules:
  0.0 608.3 jit_solution(9035415345638498831)
XLA Ops:
  19.4 23.6 %all-reduce.3 = (f32[16]{0:T(128)S(1)}, f32[16]{0:T(128)S(1)}, f32[64]{0:T(128)S(1)}) all-reduce(f32[16]{0:T(128)S(1)} %get-tuple-element.2322, f32[16]{0:T(128)S(1)} %slice_dynamic-update-slice_fusion, f32[64]{0:T(128)S(1)} %get-tuple-element.2325), channel_id=1, replica_groups=mesh['dp'=4,'seq'=16,'head'=8] {'seq'}, use_global_device_ids=true, to_apply=%add | all-reduce | flops 96 | bytes 768
  43.3 16.0 %all-gather.15.cloned.1.call-done = f32[64,128,128]{2,1,0:T(8,128)} async-done(((f32[4,128,128]{2,1,0:T(8,128)}), f32[64,128,128]{2,1,0:T(8,128)}) %all-gather.15.cloned.1.call-update) | async-done | bytes 4194320 | tf_op jit(solution)/shard_map/all_gather | solution.py:13
  62.6 8.3 %collective-permute-start.15 = (bf16[256,512]{0,1:T(8,128)(2,1)}, bf16[256,512]{0,1:T(8,128)(2,1)}, u32[]{:S(2)}, u32[]{:S(2)}) collective-permute-start(bf16[256,512]{0,1:T(8,128)(2,1)} %copy.333), channel_id=1, source_target_pairs={{8,0},{16,8},{24,16},{32,24},{40,32},{48,40},{56,48},{64,56},{72,6... | collective-permute-start | bytes 786440 | tf_op jit(solution)/shard_map/ppermute | solution.py:28
  70.9 12.9 %collective-permute-start.13 = (bf16[256,512]{0,1:T(8,128)(2,1)}, bf16[256,512]{0,1:T(8,128)(2,1)}, u32[]{:S(2)}, u32[]{:S(2)}) collective-permute-start(bf16[256,512]{0,1:T(8,128)(2,1)} %copy.333), channel_id=1, source_target_pairs={{16,0},{24,8},{32,16},{40,24},{48,32},{56,40},{64,48},{72,56},{80,... | collective-permute-start | bytes 786440 | tf_op jit(solution)/shard_map/ppermute | solution.py:28
  84.7 9.4 %collective-permute-start.14 = (bf16[256,512]{0,1:T(8,128)(2,1)}, bf16[256,512]{0,1:T(8,128)(2,1)}, u32[]{:S(2)}, u32[]{:S(2)}) collective-permute-start(bf16[256,512]{0,1:T(8,128)(2,1)} %copy.329), channel_id=1, source_target_pairs={{8,0},{16,8},{24,16},{32,24},{40,32},{48,40},{56,48},{64,56},{72,6... | collective-permute-start | bytes 786440 | tf_op jit(solution)/shard_map/ppermute | solution.py:28
  94.1 13.4 %collective-permute-start.12 = (bf16[256,512]{0,1:T(8,128)(2,1)}, bf16[256,512]{0,1:T(8,128)(2,1)}, u32[]{:S(2)}, u32[]{:S(2)}) collective-permute-start(bf16[256,512]{0,1:T(8,128)(2,1)} %copy.329), channel_id=1, source_target_pairs={{16,0},{24,8},{32,16},{40,24},{48,32},{56,40},{64,48},{72,56},{80,... | collective-permute-start | bytes 786440 | tf_op jit(solution)/shard_map/ppermute | solution.py:28
  107.4 19.6 %collective-permute-start.11 = (bf16[256,512]{0,1:T(8,128)(2,1)}, bf16[256,512]{0,1:T(8,128)(2,1)S(1)}, u32[]{:S(2)}, u32[]{:S(2)}) collective-permute-start(bf16[256,512]{0,1:T(8,128)(2,1)} %copy.333), channel_id=1, source_target_pairs={{24,0},{32,8},{40,16},{48,24},{56,32},{64,40},{72,48},{80,56},{88,... | collective-permute-start | bytes 786440 | tf_op jit(solution)/shard_map/ppermute | solution.py:28
  127.0 64.7 %all-gather.3 = s32[16,1,256]{2,1,0:T(1,128)} all-gather(s32[1,1,256]{2,1,0:T(1,128)S(1)} %bitcast.397), channel_id=1, replica_groups=mesh['dp'=4,'seq'=16,'head'=8] {'seq'}, dimensions={0}, use_global_device_ids=true | all-gather | bytes 17408 | tf_op jit(solution)/shard_map/all_gather | solution.py:88
  192.3 2.7 convert_reduce_fusion
  200.8 20.5 %while.47 = (s32[]{:T(128)}, f32[4,256]{1,0:T(4,128)S(1)}, f32[4,256]{1,0:T(4,128)S(1)}, f32[4,256,128]{2,1,0:T(8,128)S(1)}, s32[8]{0:T(128)S(1)}, /*index=5*/s3...) while((s32[]{:T(128)}, f32[4,256]{1,0:T(4,128)S(1)}, ...), condition=%wide.region_10.11_spmd.clone, body=%wide.region_5.10_spmd.clone.sunk | while | flops 275909376 | bytes 11353485 | solution.py:238
  216.3 4.9 conditional.31
  225.0 6.3 %collective-permute-start.10 = (bf16[256,512]{0,1:T(8,128)(2,1)}, bf16[256,512]{0,1:T(8,128)(2,1)S(1)}, u32[]{:S(2)}, u32[]{:S(2)}) collective-permute-start(bf16[256,512]{0,1:T(8,128)(2,1)} %copy.329), channel_id=1, source_target_pairs={{24,0},{32,8},{40,16},{48,24},{56,32},{64,40},{72,48},{80,56},{88,... | collective-permute-start | bytes 786440 | tf_op jit(solution)/shard_map/ppermute | solution.py:28
  232.4 19.6 %collective-permute-start.9 = (bf16[256,512]{0,1:T(8,128)(2,1)}, bf16[256,512]{0,1:T(8,128)(2,1)}, u32[]{:S(2)}, u32[]{:S(2)}) collective-permute-start(bf16[256,512]{0,1:T(8,128)(2,1)} %copy.333), channel_id=1, source_target_pairs={{32,0},{40,8},{48,16},{56,24},{64,32},{72,40},{80,48},{88,56},{96,... | collective-permute-start | bytes 786440 | tf_op jit(solution)/shard_map/ppermute | solution.py:28
  258.0 26.9 %collective-permute-start.5 = (bf16[256,512]{0,1:T(8,128)(2,1)}, bf16[256,512]{0,1:T(8,128)(2,1)}, u32[]{:S(2)}, u32[]{:S(2)}) collective-permute-start(bf16[256,512]{0,1:T(8,128)(2,1)} %copy.333), channel_id=1, source_target_pairs={{48,0},{56,8},{64,16},{72,24},{80,32},{88,40},{96,48},{104,56},{11... | collective-permute-start | bytes 786440 | tf_op jit(solution)/shard_map/ppermute | solution.py:28
  286.4 28.5 %while.48 = (s32[]{:T(128)}, f32[256,4,128]{0,2,1:T(8,128)}, s32[8]{0:T(128)}, s32[]{:T(128)}, s32[]{:T(128)}, /*index=5*/bf16[4096,512]{0,1:T(8,128)(2,1)}, s32...) while((s32[]{:T(128)}, f32[256,4,128]{0,2,1:T(8,128)}, ...), condition=%wide.region_15.16_spmd.clone, body=%wide.region_12.15_spmd.clone.sunk | while | flops 406979328 | bytes 9739665 | solution.py:283
  307.7 7.2 %conditional.32 = (f32[256,4,128]{0,2,1:T(8,128)}) conditional(s32[]{:T(128)} %convert_element_type.428, (s32[]{:T(128)}, bf16[4096,512]{0,1:T(8,128)(2,1)}, s32[]{:T(128)}, s32[4096]{0:T(1024)}, s32[256]{0:T(256)S(1)}, /*index=5*/bf16[256,4,128]{2,0,1:T(8,128)(2,1)S(1)}, f32[4,256]{1,0:T(4,128)}, bf16[4096,512]{0,1:T(8,128)(2,1)}, ...), branch_computations={%region_13.13_spmd, %region_14.14_spmd} | conditional | flops 406979328 | bytes 9738326 | solution.py:281
  308.7 2.5 constant_dynamic-slice_fusion.2
  311.7 3.2 fusion.23
  320.1 31.3 %collective-permute-start.4 = (bf16[256,512]{0,1:T(8,128)(2,1)}, bf16[256,512]{0,1:T(8,128)(2,1)}, u32[]{:S(2)}, u32[]{:S(2)}) collective-permute-start(bf16[256,512]{0,1:T(8,128)(2,1)} %copy.329), channel_id=1, source_target_pairs={{48,0},{56,8},{64,16},{72,24},{80,32},{88,40},{96,48},{104,56},{11... | collective-permute-start | bytes 786440 | tf_op jit(solution)/shard_map/ppermute | solution.py:28
  355.4 2.0 collective-permute-start.1
  361.5 42.2 %all_gather.55 = f32[4,4096]{0,1:T(8,128)S(1)} all-gather(f32[4,256]{0,1:T(8,128)S(1)} %bitcast.376), channel_id=1, replica_groups=mesh['dp'=4,'seq'=16,'head'=8] {'seq'}, dimensions={1}, use_global_device_ids=true | all-gather | bytes 69632 | tf_op jit(solution)/shard_map/all_gather | solution.py:244
  403.7 22.0 %all_gather.54 = f32[4,4096]{1,0:T(4,128)} all-gather(f32[4,256]{1,0:T(4,128)S(1)} %copy-done.30), channel_id=1, replica_groups=mesh['dp'=4,'seq'=16,'head'=8] {'seq'}, dimensions={1}, use_global_device_ids=true | all-gather | bytes 69632 | tf_op jit(solution)/shard_map/all_gather | solution.py:243
  426.6 9.7 %conditional.18 = (f32[256,4,128]{2,0,1:T(8,128)S(1)}, f32[256,4,128]{2,0,1:T(8,128)S(1)}) conditional(s32[]{:T(128)} %convert_element_type.265, (s32[256]{0:T(256)S(1)}, s32[]{:T(128)}, s32[256]{0:T(256)S(1)}, s32[4096]{0:T(1024)}, bf16[256,4,128]{0,2,1:T(8,128)(2,1)}, /*index=5*/bf16[256,4,128]{0,2,1:T(8,128)(2,1)S(1)}, f32[4,4096]{1,0:T(4,128)}, ...), branch_computations={%region_17.18_spmd, %region_18.19_spmd} | conditional | flops 271122688 | bytes 10255450 | solution.py:332
  428.9 2.4 fusion.37
  432.3 2.1 fusion.42
  436.3 8.6 %conditional.19 = ((f32[256,4,128]{2,0,1:T(8,128)S(1)}, f32[256,4,128]{2,0,1:T(8,128)S(1)})) conditional(s32[]{:T(128)} %convert_element_type.264, (s32[256]{0:T(256)S(1)}, s32[]{:T(128)}, s32[256]{0:T(256)S(1)}, s32[4096]{0:T(1024)}, bf16[256,4,128]{0,2,1:T(8,128)(2,1)}, /*index=5*/bf16[256,4,128]{0,2,1:T(8,128)(2,1)}, f32[4,4096]{1,0:T(4,128)}, ...), branch_computations={%region_19.20_spmd, %region_20.21_spmd} | conditional | flops 271122688 | bytes 7109702 | solution.py:332
  438.6 2.5 fusion.50
  441.1 2.1 fusion.55
  444.9 8.6 %conditional.20 = ((f32[256,4,128]{2,0,1:T(8,128)S(1)}, f32[256,4,128]{2,0,1:T(8,128)S(1)})) conditional(s32[]{:T(128)} %convert_element_type.263, (s32[256]{0:T(256)S(1)}, s32[]{:T(128)}, s32[256]{0:T(256)S(1)}, s32[4096]{0:T(1024)}, bf16[256,4,128]{0,2,1:T(8,128)(2,1)}, /*index=5*/bf16[256,4,128]{0,2,1:T(8,128)(2,1)}, f32[4,4096]{1,0:T(4,128)}, ...), branch_computations={%region_21.22_spmd, %region_22.23_spmd} | conditional | flops 271122688 | bytes 7109702 | solution.py:332
  447.2 2.5 fusion.63
  449.7 2.1 fusion.68
  453.5 8.8 %conditional.21 = ((f32[256,4,128]{2,0,1:T(8,128)S(1)}, f32[256,4,128]{2,0,1:T(8,128)S(1)})) conditional(s32[]{:T(128)} %convert_element_type.262, (s32[256]{0:T(256)S(1)}, s32[]{:T(128)}, s32[256]{0:T(256)S(1)}, s32[4096]{0:T(1024)}, bf16[256,4,128]{0,2,1:T(8,128)(2,1)}, /*index=5*/bf16[256,4,128]{0,2,1:T(8,128)(2,1)}, f32[4,4096]{1,0:T(4,128)}, ...), branch_computations={%region_23.24_spmd, %region_24.25_spmd} | conditional | flops 271122688 | bytes 7109702 | solution.py:332
  456.0 2.5 fusion.76
  458.5 2.1 fusion.81
  462.3 8.6 %conditional.22 = ((f32[256,4,128]{2,0,1:T(8,128)S(1)}, f32[256,4,128]{2,0,1:T(8,128)S(1)})) conditional(s32[]{:T(128)} %convert_element_type.261, (s32[256]{0:T(256)S(1)}, s32[]{:T(128)}, s32[256]{0:T(256)S(1)}, s32[4096]{0:T(1024)}, bf16[256,4,128]{0,2,1:T(8,128)(2,1)}, /*index=5*/bf16[256,4,128]{0,2,1:T(8,128)(2,1)}, f32[4,4096]{1,0:T(4,128)}, ...), branch_computations={%region_25.26_spmd, %region_26.27_spmd} | conditional | flops 271122688 | bytes 7109702 | solution.py:332
  464.6 2.5 fusion.89
  467.1 2.1 fusion.94
  470.9 8.6 %conditional.23 = ((f32[256,4,128]{2,0,1:T(8,128)S(1)}, f32[256,4,128]{2,0,1:T(8,128)S(1)})) conditional(s32[]{:T(128)} %convert_element_type.260, (s32[256]{0:T(256)S(1)}, s32[]{:T(128)}, s32[256]{0:T(256)S(1)}, s32[4096]{0:T(1024)}, bf16[256,4,128]{0,2,1:T(8,128)(2,1)}, /*index=5*/bf16[256,4,128]{0,2,1:T(8,128)(2,1)}, f32[4,4096]{1,0:T(4,128)}, ...), branch_computations={%region_27.28_spmd, %region_28.29_spmd} | conditional | flops 271122688 | bytes 7109702 | solution.py:332
  473.2 2.5 fusion.102
  475.7 2.1 fusion.107
  479.5 8.6 %conditional.24 = ((f32[256,4,128]{2,0,1:T(8,128)S(1)}, f32[256,4,128]{2,0,1:T(8,128)S(1)})) conditional(s32[]{:T(128)} %convert_element_type.259, (s32[256]{0:T(256)S(1)}, s32[]{:T(128)}, s32[256]{0:T(256)S(1)}, s32[4096]{0:T(1024)}, bf16[256,4,128]{0,2,1:T(8,128)(2,1)}, /*index=5*/bf16[256,4,128]{0,2,1:T(8,128)(2,1)}, f32[4,4096]{1,0:T(4,128)}, ...), branch_computations={%region_29.30_spmd, %region_30.31_spmd} | conditional | flops 271122688 | bytes 7109702 | solution.py:332
  481.8 2.5 fusion.115
  484.3 2.1 fusion.120
  488.1 8.6 %conditional.25 = ((f32[256,4,128]{2,0,1:T(8,128)S(1)}, f32[256,4,128]{2,0,1:T(8,128)S(1)})) conditional(s32[]{:T(128)} %convert_element_type.258, (s32[256]{0:T(256)S(1)}, s32[]{:T(128)}, s32[256]{0:T(256)S(1)}, s32[4096]{0:T(1024)}, bf16[256,4,128]{0,2,1:T(8,128)(2,1)}, /*index=5*/bf16[256,4,128]{0,2,1:T(8,128)(2,1)}, f32[4,4096]{1,0:T(4,128)}, ...), branch_computations={%region_31.32_spmd, %region_32.33_spmd} | conditional | flops 271122688 | bytes 7109702 | solution.py:332
  490.4 2.5 fusion.128
  492.9 2.1 fusion.133
  496.8 7.6 %conditional.26 = (bf16[256,512]{1,0:T(8,128)(2,1)S(1)}, bf16[256,512]{1,0:T(8,128)(2,1)S(1)}) conditional(s32[]{:T(128)} %convert_element_type.257, (s32[256]{0:T(256)S(1)}, s32[]{:T(128)}, s32[256]{0:T(256)S(1)}, s32[4096]{0:T(1024)}, bf16[256,512]{0,1:T(8,128)(2,1)}, /*index=5*/bf16[256,4,128]{0,2,1:T(8,128)(2,1)}, f32[4,4096]{1,0:T(4,128)}, ...), branch_computations={%region_33.34_spmd, %region_34.35_spmd} | conditional | flops 271384832 | bytes 10779738
  505.1 92.7 %while.45 = (s32[]{:T(128)}, f32[4,128,128]{2,1,0:T(8,128)S(1)}, f32[]{:T(128)}, s32[]{:T(128)}, f32[16]{0:T(128)S(1)}, /*index=5*/f32[16]{0:T(128)S(1)}, f32[16...) while((s32[]{:T(128)}, f32[4,128,128]{2,1,0:T(8,128)S(1)}, ...), condition=%wide.region_1.2_spmd, body=%wide.region_0.1_spmd.sunk | while | flops 262154 | bytes 786708 | solution.py:22
  (375 shorter events, 158.8 us)
Async XLA Ops:
  7.2 53.5 %copy-start = (bf16[256,512]{1,0:T(8,128)(2,1)S(1)}, bf16[256,512]{1,0:T(8,128)(2,1)}, u32[]{:S(2)}) copy-start(bf16[256,512]{1,0:T(8,128)(2,1)} %param.43) | copy-start | bytes 786436
  7.2 12.1 %copy-start.32 = (f32[4]{0:T(128)S(1)}, f32[4]{0:T(128)}, u32[]{:S(2)}) copy-start(f32[4]{0:T(128)} %param.44) | copy-start | bytes 52
  7.2 8.8 %copy-start.22 = (bf16[256,512]{1,0:T(8,128)(2,1)S(1)}, bf16[256,512]{1,0:T(8,128)(2,1)}, u32[]{:S(2)}) copy-start(bf16[256,512]{1,0:T(8,128)(2,1)} %param.48) | copy-start | bytes 786436
  7.2 9.8 %copy-start.23 = (bf16[256,512]{1,0:T(8,128)(2,1)S(1)}, bf16[256,512]{1,0:T(8,128)(2,1)}, u32[]{:S(2)}) copy-start(bf16[256,512]{1,0:T(8,128)(2,1)} %param.47) | copy-start | bytes 786436
  7.2 35.9 %copy-start.12 = (bf16[256,512]{1,0:T(8,128)(2,1)S(1)}, bf16[256,512]{1,0:T(8,128)(2,1)}, u32[]{:S(2)}) copy-start(bf16[256,512]{1,0:T(8,128)(2,1)} %param.42) | copy-start | bytes 786436
  7.2 52.0 %all-gather.15.cloned.1.call-start = ((), (), s32[]{:S(2)}) async-start(), calls=%async_computation.3 | async-start | bytes 4456448 | tf_op jit(solution)/shard_map/all_gather | solution.py:13
  7.3 35.9 %copy-start.34 = (f32[256]{0:T(256)}, f32[256]{0:T(256)S(1)}, u32[]{:S(2)}) copy-start(f32[256]{0:T(256)S(1)} %convert_negate_fusion) | copy-start | bytes 3076
  13.0 218.3 %copy-start.7 = (bf16[256,512]{0,1:T(8,128)(2,1)}, bf16[256,512]{0,1:T(8,128)(2,1)S(1)}, u32[]{:S(2)}) copy-start(bf16[256,512]{0,1:T(8,128)(2,1)S(1)} %copy.484) | copy-start | bytes 786436
  14.2 184.7 %copy-start.9 = (bf16[256,512]{0,1:T(8,128)(2,1)}, bf16[256,512]{0,1:T(8,128)(2,1)S(1)}, u32[]{:S(2)}) copy-start(bf16[256,512]{0,1:T(8,128)(2,1)S(1)} %copy.485) | copy-start | bytes 786436
  16.0 184.7 %all-gather.11.cloned.1.call-start = ((), (), s32[]{:S(2)}) async-start(), calls=%async_computation.1 | async-start | bytes 4456448 | tf_op jit(solution)/shard_map/all_gather | solution.py:177
  16.9 183.8 %all-gather.9.cloned.1.call-start = ((), (), s32[]{:S(2)}) async-start(), calls=%async_computation | async-start | bytes 4456448 | tf_op jit(solution)/shard_map/all_gather | solution.py:176
  17.8 486.5 %all-gather.13.cloned.1.call-start = ((), (), s32[]{:S(2)}) async-start(), calls=%async_computation.2 | async-start | bytes 4456448 | tf_op jit(solution)/shard_map/all_gather | solution.py:13
  43.2 17.5 %copy-start.13 = (bf16[256,512]{0,1:T(8,128)(2,1)}, bf16[256,512]{0,1:T(8,128)(2,1)S(1)}, u32[]{:S(2)}) copy-start(bf16[256,512]{0,1:T(8,128)(2,1)S(1)} %copy.512) | copy-start | bytes 786436
  59.3 24.5 %copy-start.25 = (bf16[256,512]{1,0:T(8,128)(2,1)S(1)}, bf16[256,512]{1,0:T(8,128)(2,1)}, u32[]{:S(2)}) copy-start(bf16[256,512]{1,0:T(8,128)(2,1)} %param.46) | copy-start | bytes 786436
  59.4 34.7 %copy-start.31 = (f32[16,4]{1,0:T(8,128)}, f32[16,4]{1,0:T(8,128)S(1)}, u32[]{:S(2)}) copy-start(f32[16,4]{1,0:T(8,128)S(1)} %get-tuple-element.2858) | copy-start | bytes 772
  59.4 139.9 %copy-start.38 = (f32[16]{0:T(128)}, f32[16]{0:T(128)S(1)}, u32[]{:S(2)}) copy-start(f32[16]{0:T(128)S(1)} %get-tuple-element.2860) | copy-start | bytes 196
  62.6 162.4 %collective-permute-start.15 = (bf16[256,512]{0,1:T(8,128)(2,1)}, bf16[256,512]{0,1:T(8,128)(2,1)}, u32[]{:S(2)}, u32[]{:S(2)}) collective-permute-start(bf16[256,512]{0,1:T(8,128)(2,1)} %copy.333), channel_id=1, source_target_pairs={{8,0},{16,8},{24,16},{32,24},{40,32},{48,40},{56,48},{64,56},{72,6... | collective-permute-start | bytes 786440 | tf_op jit(solution)/shard_map/ppermute | solution.py:28
  70.9 181.1 %collective-permute-start.13 = (bf16[256,512]{0,1:T(8,128)(2,1)}, bf16[256,512]{0,1:T(8,128)(2,1)}, u32[]{:S(2)}, u32[]{:S(2)}) collective-permute-start(bf16[256,512]{0,1:T(8,128)(2,1)} %copy.333), channel_id=1, source_target_pairs={{16,0},{24,8},{32,16},{40,24},{48,32},{56,40},{64,48},{72,56},{80,... | collective-permute-start | bytes 786440 | tf_op jit(solution)/shard_map/ppermute | solution.py:28
  84.7 147.7 %collective-permute-start.14 = (bf16[256,512]{0,1:T(8,128)(2,1)}, bf16[256,512]{0,1:T(8,128)(2,1)}, u32[]{:S(2)}, u32[]{:S(2)}) collective-permute-start(bf16[256,512]{0,1:T(8,128)(2,1)} %copy.329), channel_id=1, source_target_pairs={{8,0},{16,8},{24,16},{32,24},{40,32},{48,40},{56,48},{64,56},{72,6... | collective-permute-start | bytes 786440 | tf_op jit(solution)/shard_map/ppermute | solution.py:28
  94.1 160.0 %collective-permute-start.12 = (bf16[256,512]{0,1:T(8,128)(2,1)}, bf16[256,512]{0,1:T(8,128)(2,1)}, u32[]{:S(2)}, u32[]{:S(2)}) collective-permute-start(bf16[256,512]{0,1:T(8,128)(2,1)} %copy.329), channel_id=1, source_target_pairs={{16,0},{24,8},{32,16},{40,24},{48,32},{56,40},{64,48},{72,56},{80,... | collective-permute-start | bytes 786440 | tf_op jit(solution)/shard_map/ppermute | solution.py:28
  107.4 148.6 %collective-permute-start.11 = (bf16[256,512]{0,1:T(8,128)(2,1)}, bf16[256,512]{0,1:T(8,128)(2,1)S(1)}, u32[]{:S(2)}, u32[]{:S(2)}) collective-permute-start(bf16[256,512]{0,1:T(8,128)(2,1)} %copy.333), channel_id=1, source_target_pairs={{24,0},{32,8},{40,16},{48,24},{56,32},{64,40},{72,48},{80,56},{88,... | collective-permute-start | bytes 786440 | tf_op jit(solution)/shard_map/ppermute | solution.py:28
  199.3 32.0 %copy-start.5 = (f32[4,256,256]{2,1,0:T(8,128)}, f32[4,256,256]{2,1,0:T(8,128)S(1)}, u32[]{:S(2)}) copy-start(f32[4,256,256]{2,1,0:T(8,128)S(1)} %convolution_multiply_fusion.9) | copy-start | bytes 3145732
  224.0 62.4 %copy-start.16 = (f32[256,4]{1,0:T(8,128)}, f32[256,4]{1,0:T(8,128)S(1)}, u32[]{:S(2)}) copy-start(f32[256,4]{1,0:T(8,128)S(1)} %copy.482) | copy-start | bytes 12292
  225.0 33.0 %collective-permute-start.10 = (bf16[256,512]{0,1:T(8,128)(2,1)}, bf16[256,512]{0,1:T(8,128)(2,1)S(1)}, u32[]{:S(2)}, u32[]{:S(2)}) collective-permute-start(bf16[256,512]{0,1:T(8,128)(2,1)} %copy.329), channel_id=1, source_target_pairs={{24,0},{32,8},{40,16},{48,24},{56,32},{64,40},{72,48},{80,56},{88,... | collective-permute-start | bytes 786440 | tf_op jit(solution)/shard_map/ppermute | solution.py:28
  232.4 87.7 %collective-permute-start.9 = (bf16[256,512]{0,1:T(8,128)(2,1)}, bf16[256,512]{0,1:T(8,128)(2,1)}, u32[]{:S(2)}, u32[]{:S(2)}) collective-permute-start(bf16[256,512]{0,1:T(8,128)(2,1)} %copy.333), channel_id=1, source_target_pairs={{32,0},{40,8},{48,16},{56,24},{64,32},{72,40},{80,48},{88,56},{96,... | collective-permute-start | bytes 786440 | tf_op jit(solution)/shard_map/ppermute | solution.py:28
  252.0 99.4 %collective-permute-start.8 = (bf16[256,512]{0,1:T(8,128)(2,1)}, bf16[256,512]{0,1:T(8,128)(2,1)}, u32[]{:S(2)}, u32[]{:S(2)}) collective-permute-start(bf16[256,512]{0,1:T(8,128)(2,1)} %copy.329), channel_id=1, source_target_pairs={{32,0},{40,8},{48,16},{56,24},{64,32},{72,40},{80,48},{88,56},{96,... | collective-permute-start | bytes 786440 | tf_op jit(solution)/shard_map/ppermute | solution.py:28
  254.0 99.4 %collective-permute-start.7 = (bf16[256,512]{0,1:T(8,128)(2,1)}, bf16[256,512]{0,1:T(8,128)(2,1)}, u32[]{:S(2)}, u32[]{:S(2)}) collective-permute-start(bf16[256,512]{0,1:T(8,128)(2,1)} %copy.333), channel_id=1, source_target_pairs={{40,0},{48,8},{56,16},{64,24},{72,32},{80,40},{88,48},{96,56},{104... | collective-permute-start | bytes 786440 | tf_op jit(solution)/shard_map/ppermute | solution.py:28
  256.0 30.3 %copy-start.20 = (bf16[256,512]{0,1:T(8,128)(2,1)}, bf16[256,512]{0,1:T(8,128)(2,1)S(1)}, u32[]{:S(2)}) copy-start(bf16[256,512]{0,1:T(8,128)(2,1)S(1)} %collective-permute-done.11) | copy-start | bytes 786436
  256.0 99.4 %collective-permute-start.6 = (bf16[256,512]{0,1:T(8,128)(2,1)}, bf16[256,512]{0,1:T(8,128)(2,1)}, u32[]{:S(2)}, u32[]{:S(2)}) collective-permute-start(bf16[256,512]{0,1:T(8,128)(2,1)} %copy.329), channel_id=1, source_target_pairs={{40,0},{48,8},{56,16},{64,24},{72,32},{80,40},{88,48},{96,56},{104... | collective-permute-start | bytes 786440 | tf_op jit(solution)/shard_map/ppermute | solution.py:28
  258.0 28.3 %copy-start.28 = (bf16[256,512]{0,1:T(8,128)(2,1)}, bf16[256,512]{0,1:T(8,128)(2,1)S(1)}, u32[]{:S(2)}) copy-start(bf16[256,512]{0,1:T(8,128)(2,1)S(1)} %collective-permute-done.10) | copy-start | bytes 786436
  258.0 99.4 %collective-permute-start.5 = (bf16[256,512]{0,1:T(8,128)(2,1)}, bf16[256,512]{0,1:T(8,128)(2,1)}, u32[]{:S(2)}, u32[]{:S(2)}) collective-permute-start(bf16[256,512]{0,1:T(8,128)(2,1)} %copy.333), channel_id=1, source_target_pairs={{48,0},{56,8},{64,16},{72,24},{80,32},{88,40},{96,48},{104,56},{11... | collective-permute-start | bytes 786440 | tf_op jit(solution)/shard_map/ppermute | solution.py:28
  314.9 44.5 %copy-start.3 = (f32[4,256,256]{2,1,0:T(8,128)S(1)}, f32[4,256,256]{2,1,0:T(8,128)}, u32[]{:S(2)}) copy-start(f32[4,256,256]{2,1,0:T(8,128)} %convolution_multiply_fusion.10) | copy-start | bytes 3145732
  314.9 44.5 %copy-start.10 = (bf16[256,512]{0,1:T(8,128)(2,1)S(1)}, bf16[256,512]{0,1:T(8,128)(2,1)}, u32[]{:S(2)}) copy-start(bf16[256,512]{0,1:T(8,128)(2,1)} %copy-done.9) | copy-start | bytes 786436
  316.9 43.7 %copy-start.19 = (bf16[4,256,128]{1,2,0:T(8,128)(2,1)S(1)}, bf16[4,256,128]{1,2,0:T(8,128)(2,1)}, u32[]{:S(2)}) copy-start(bf16[4,256,128]{1,2,0:T(8,128)(2,1)} %get-tuple-element.2290) | copy-start | bytes 786436
  318.8 42.7 %copy-start.17 = (f32[256,4]{1,0:T(8,128)S(1)}, f32[256,4]{1,0:T(8,128)}, u32[]{:S(2)}) copy-start(f32[256,4]{1,0:T(8,128)} %copy-done.16) | copy-start | bytes 12292
  320.1 159.4 %collective-permute-start.4 = (bf16[256,512]{0,1:T(8,128)(2,1)}, bf16[256,512]{0,1:T(8,128)(2,1)}, u32[]{:S(2)}, u32[]{:S(2)}) collective-permute-start(bf16[256,512]{0,1:T(8,128)(2,1)} %copy.329), channel_id=1, source_target_pairs={{48,0},{56,8},{64,16},{72,24},{80,32},{88,40},{96,48},{104,56},{11... | collective-permute-start | bytes 786440 | tf_op jit(solution)/shard_map/ppermute | solution.py:28
  351.4 136.7 %collective-permute-start.3 = (bf16[256,512]{0,1:T(8,128)(2,1)}, bf16[256,512]{0,1:T(8,128)(2,1)}, u32[]{:S(2)}, u32[]{:S(2)}) collective-permute-start(bf16[256,512]{0,1:T(8,128)(2,1)} %copy.333), channel_id=1, source_target_pairs={{56,0},{64,8},{72,16},{80,24},{88,32},{96,40},{104,48},{112,56},{1... | collective-permute-start | bytes 786440 | tf_op jit(solution)/shard_map/ppermute | solution.py:28
  353.4 134.7 %collective-permute-start.2 = (bf16[256,512]{0,1:T(8,128)(2,1)}, bf16[256,512]{0,1:T(8,128)(2,1)}, u32[]{:S(2)}, u32[]{:S(2)}) collective-permute-start(bf16[256,512]{0,1:T(8,128)(2,1)} %copy.329), channel_id=1, source_target_pairs={{56,0},{64,8},{72,16},{80,24},{88,32},{96,40},{104,48},{112,56},{1... | collective-permute-start | bytes 786440 | tf_op jit(solution)/shard_map/ppermute | solution.py:28
  355.4 141.3 %collective-permute-start.1 = (bf16[256,512]{0,1:T(8,128)(2,1)}, bf16[256,512]{0,1:T(8,128)(2,1)}, u32[]{:S(2)}, u32[]{:S(2)}) collective-permute-start(bf16[256,512]{0,1:T(8,128)(2,1)} %copy.333), channel_id=1, source_target_pairs={{64,0},{72,8},{80,16},{88,24},{96,32},{104,40},{112,48},{120,56},{... | collective-permute-start | bytes 786440 | tf_op jit(solution)/shard_map/ppermute | solution.py:28
  357.4 139.3 %collective-permute-start = (bf16[256,512]{0,1:T(8,128)(2,1)}, bf16[256,512]{0,1:T(8,128)(2,1)}, u32[]{:S(2)}, u32[]{:S(2)}) collective-permute-start(bf16[256,512]{0,1:T(8,128)(2,1)} %copy.329), channel_id=1, source_target_pairs={{64,0},{72,8},{80,16},{88,24},{96,32},{104,40},{112,48},{120,56},{... | collective-permute-start | bytes 786440 | tf_op jit(solution)/shard_map/ppermute | solution.py:28
  359.8 44.0 %copy-start.30 = (f32[4,256]{1,0:T(4,128)S(1)}, f32[4,256]{1,0:T(4,128)}, u32[]{:S(2)}) copy-start(f32[4,256]{1,0:T(4,128)} %get-tuple-element.2857) | copy-start | bytes 12292
  359.8 66.8 %copy-start.1 = (bf16[256,512]{0,1:T(8,128)(2,1)S(1)}, bf16[256,512]{0,1:T(8,128)(2,1)}, u32[]{:S(2)}) copy-start(bf16[256,512]{0,1:T(8,128)(2,1)} %copy.330) | copy-start | bytes 786436
  359.8 66.8 %copy-start.18 = (bf16[256,512]{0,1:T(8,128)(2,1)S(1)}, bf16[256,512]{0,1:T(8,128)(2,1)}, u32[]{:S(2)}) copy-start(bf16[256,512]{0,1:T(8,128)(2,1)} %copy.328) | copy-start | bytes 786436
  496.7 7.7 %copy-start.37 = (f32[16]{0:T(128)S(1)}, f32[16]{0:T(128)}, u32[]{:S(2)}) copy-start(f32[16]{0:T(128)} %copy-done.36) | copy-start | bytes 196
  504.4 93.4 %copy-start.33 = (f32[4]{0:T(128)S(1)}, f32[4]{0:T(128)}, u32[]{:S(2)}) copy-start(f32[4]{0:T(128)} %param.44) | copy-start | bytes 52
  504.5 93.4 %copy-start.35 = (f32[256]{0:T(256)S(1)}, f32[256]{0:T(256)}, u32[]{:S(2)}) copy-start(f32[256]{0:T(256)} %copy-done.34) | copy-start | bytes 3076
  504.5 93.5 %copy-start.11 = (bf16[256,512]{0,1:T(8,128)(2,1)S(1)}, bf16[256,512]{0,1:T(8,128)(2,1)}, u32[]{:S(2)}) copy-start(bf16[256,512]{0,1:T(8,128)(2,1)} %copy-done.9) | copy-start | bytes 786436
  504.5 93.9 %copy-start.8 = (bf16[256,512]{0,1:T(8,128)(2,1)S(1)}, bf16[256,512]{0,1:T(8,128)(2,1)}, u32[]{:S(2)}) copy-start(bf16[256,512]{0,1:T(8,128)(2,1)} %copy-done.7) | copy-start | bytes 786436
  (12 other events, 26.6 us)
Sparse Core Ops, SparseCore 0:
  16.1 43.1 all-gather.14
  61.3 50.4 all-gather.10
  114.4 61.8 all-gather.8
  178.9 45.5 all-gather.12
where the time goes:
time: 613 us; the launch traced here: 608 us
  starting transfers between devices  162 us (26%)
  blocking collectives  152 us (25%)
  local copies, waits for them, and re-layouts  94.5 us (15%)
  loops' own time  70.5 us (12%)
  matrix products  68.5 us (11%)
  other arithmetic  28.5 us (5%)
  waiting for transfers between devices  16.1 us (3%)
  between operations  16 us (3%)
    ppermute x16, starting transfers between devices, from_behind(): lax.ppermute(value, axis, [(source, source + steps) for source in range(f...  162 us
    all_gather x1, blocking collectives, per_device(): all_ids = lax.all_gather(doc_ids, 'seq', axis=0, tiled=True)  64.7 us
    another operation x2, loops' own time, entering(): return lax.fori_loop(0, ahead, one, state)  47.9 us
    all_gather x1, blocking collectives, per_device(): lax.all_gather(delta, 'seq', axis=1, tiled=True)  42.2 us
    unnamed x1, blocking collectives  23.6 us
    all_gather x1, blocking collectives, per_device(): lax.all_gather(lse, 'seq', axis=1, tiled=True)  22 us
    dot_general x9, matrix products, key_terms(): jnp.einsum('thd,shd->hts', piece_query, soft_keys, preferred_element_type...  21.4 us
    dynamic_slice x30, local copies, waits for them, and re-layouts, one(): lax.dynamic_index_in_dim(a, source, 0, False)  18.4 us
  transfers between devices with their start and end apart: 20, of which 1 were waited for; matrix products, arithmetic and copies ran while one was open for 22% of the time, Pallas kernels for 0%

commit v1 on v0

--- a/solution.py
+++ b/solution.py
@@ -85,7 +85,9 @@
     total_rows = tok_rows * shards
     offset = lax.axis_index("seq") * tok_rows
     last_pos = offset + tok_rows - 1
-    all_ids = lax.all_gather(doc_ids, "seq", axis=0, tiled=True)
+    all_ids = jnp.concatenate(
+        lax.all_to_all(jnp.stack([doc_ids] * lax.axis_size("seq")), "seq", 0, 0), axis=0
+    )
     positions = offset + jnp.arange(tok_rows, dtype=jnp.int32)
     own_ids = doc_ids.astype(jnp.float32)
     within_segment_position = jnp.arange(tok_rows, dtype=jnp.int32)

time: 613 us -> 591 us (0.964)
  blocking collectives: 152 us -> 90.6 us
  starting transfers between devices: 162 us -> 191 us
  waiting for transfers between devices: 16.1 us -> 26.5 us
    all_gather x1 -> x0, blocking collectives: 64.7 us -> none  [per_device(): all_ids = lax.all_gather(doc_ids, 'seq', axis=0, tiled=True)]
    all_to_all x0 -> x1, starting transfers between devices: none -> 38.6 us  [per_device(): lax.all_to_all(jnp.stack([doc_ids] * lax.axis_size('seq')), 'seq', 0, 0)]
    all_to_all x0 -> x1, waiting for transfers between devices: none -> 10.3 us  [per_device(): lax.all_to_all(jnp.stack([doc_ids] * lax.axis_size('seq')), 'seq', 0, 0)]
    ppermute x16, starting transfers between devices: 162 us -> 152 us  [from_behind(): lax.ppermute(value, axis, [(source, source + steps) for source in range(f...]
  transfers between devices with their start and end apart: 20 -> 21, of which waited for: 1 -> 2; matrix products, arithmetic and copies ran while one was open for 22% -> 23% of each run, Pallas kernels for 0% -> 0%
where the time goes in v1:
time: 591 us; the launch traced here: 586 us
  starting transfers between devices  191 us (32%)
  local copies, waits for them, and re-layouts  94.7 us (16%)
  blocking collectives  90.6 us (15%)
  loops' own time  70.4 us (12%)
  matrix products  68.6 us (12%)
  other arithmetic  28.4 us (5%)
  waiting for transfers between devices  26.5 us (4%)
  between operations  16 us (3%)
    ppermute x16, starting transfers between devices, from_behind(): lax.ppermute(value, axis, [(source, source + steps) for source in range(f...  152 us
    another operation x2, loops' own time, entering(): return lax.fori_loop(0, ahead, one, state)  48.1 us
    all_gather x1, blocking collectives, per_device(): lax.all_gather(delta, 'seq', axis=1, tiled=True)  46.9 us
    all_to_all x1, starting transfers between devices, per_device(): lax.all_to_all(jnp.stack([doc_ids] * lax.axis_size('seq')), 'seq', 0, 0)  38.6 us
    unnamed x1, blocking collectives  23.6 us
    dot_general x9, matrix products, key_terms(): jnp.einsum('thd,shd->hts', piece_query, soft_keys, preferred_element_type...  21.5 us
    all_gather x1, blocking collectives, per_device(): lax.all_gather(lse, 'seq', axis=1, tiled=True)  20 us
    dot_general x9, matrix products, key_terms(): jnp.einsum('hts,thd->shd', dlogit, piece_query, preferred_element_type=jn...  18.4 us
  transfers between devices with their start and end apart: 21, of which 2 were waited for; matrix products, arithmetic and copies ran while one was open for 23% of the time, Pallas kernels for 0%

profile of v1, /device:TPU:449, one launch (start us, length us, event | category | flops | bytes accessed | tf_op | source)
XLA Modules:
  0.0 585.8 jit_solution(12118323124451201223)
XLA Ops:
  19.4 23.6 %all-reduce.3 = (f32[16]{0:T(128)S(1)}, f32[16]{0:T(128)S(1)}, f32[64]{0:T(128)S(1)}) all-reduce(f32[16]{0:T(128)S(1)} %get-tuple-element.2754, f32[16]{0:T(128)S(1)} %slice_dynamic-update-slice_fusion, f32[64]{0:T(128)S(1)} %get-tuple-element.2757), channel_id=1, replica_groups=mesh['dp'=4,'seq'=16,'head'=8] {'seq'}, use_global_device_ids=true, to_apply=%add | all-reduce | flops 96 | bytes 768
  43.2 16.0 %all-gather.14.cloned.1.call-done = f32[64,128,128]{2,1,0:T(8,128)} async-done(((f32[4,128,128]{2,1,0:T(8,128)}), f32[64,128,128]{2,1,0:T(8,128)}) %all-gather.14.cloned.1.call-update) | async-done | bytes 4194320 | tf_op jit(solution)/shard_map/all_gather | solution.py:13
  62.6 8.4 %collective-permute-start.15 = (bf16[256,512]{0,1:T(8,128)(2,1)}, bf16[256,512]{0,1:T(8,128)(2,1)}, u32[]{:S(2)}, u32[]{:S(2)}) collective-permute-start(bf16[256,512]{0,1:T(8,128)(2,1)} %copy.720), channel_id=1, source_target_pairs={{8,0},{16,8},{24,16},{32,24},{40,32},{48,40},{56,48},{64,56},{72,6... | collective-permute-start | bytes 786440 | tf_op jit(solution)/shard_map/ppermute | solution.py:28
  71.0 13.0 %collective-permute-start.13 = (bf16[256,512]{0,1:T(8,128)(2,1)}, bf16[256,512]{0,1:T(8,128)(2,1)}, u32[]{:S(2)}, u32[]{:S(2)}) collective-permute-start(bf16[256,512]{0,1:T(8,128)(2,1)} %copy.720), channel_id=1, source_target_pairs={{16,0},{24,8},{32,16},{40,24},{48,32},{56,40},{64,48},{72,56},{80,... | collective-permute-start | bytes 786440 | tf_op jit(solution)/shard_map/ppermute | solution.py:28
  84.8 9.4 %collective-permute-start.14 = (bf16[256,512]{0,1:T(8,128)(2,1)}, bf16[256,512]{0,1:T(8,128)(2,1)}, u32[]{:S(2)}, u32[]{:S(2)}) collective-permute-start(bf16[256,512]{0,1:T(8,128)(2,1)} %copy.716), channel_id=1, source_target_pairs={{8,0},{16,8},{24,16},{32,24},{40,32},{48,40},{56,48},{64,56},{72,6... | collective-permute-start | bytes 786440 | tf_op jit(solution)/shard_map/ppermute | solution.py:28
  94.1 13.4 %collective-permute-start.12 = (bf16[256,512]{0,1:T(8,128)(2,1)}, bf16[256,512]{0,1:T(8,128)(2,1)}, u32[]{:S(2)}, u32[]{:S(2)}) collective-permute-start(bf16[256,512]{0,1:T(8,128)(2,1)} %copy.716), channel_id=1, source_target_pairs={{16,0},{24,8},{32,16},{40,24},{48,32},{56,40},{64,48},{72,56},{80,... | collective-permute-start | bytes 786440 | tf_op jit(solution)/shard_map/ppermute | solution.py:28
  107.5 19.6 %collective-permute-start.11 = (bf16[256,512]{0,1:T(8,128)(2,1)}, bf16[256,512]{0,1:T(8,128)(2,1)S(1)}, u32[]{:S(2)}, u32[]{:S(2)}) collective-permute-start(bf16[256,512]{0,1:T(8,128)(2,1)} %copy.720), channel_id=1, source_target_pairs={{24,0},{32,8},{40,16},{48,24},{56,32},{64,40},{72,48},{80,56},{88,... | collective-permute-start | bytes 786440 | tf_op jit(solution)/shard_map/ppermute | solution.py:28
  127.7 38.6 %all-to-all-start = ((s32[16,1,256]{2,1,0:T(1,128)}), s32[16,1,256]{2,1,0:T(1,128)}, u32[]{:S(2)}, u32[]{:S(2)}) async-start(s32[16,1,256]{2,1,0:T(1,128)} %stack.2), calls=%async_computation | async-start | bytes 32768 | tf_op jit(solution)/shard_map/all_to_all | solution.py:89
  171.9 10.3 %all-to-all-done = s32[16,1,256]{2,1,0:T(1,128)} async-done(((s32[16,1,256]{2,1,0:T(1,128)}), s32[16,1,256]{2,1,0:T(1,128)}, u32[]{:S(2)}, u32[]{:S(2)}) %all-to-all-start) | async-done | bytes 16416 | tf_op jit(solution)/shard_map/all_to_all | solution.py:89
  182.2 2.7 convert_reduce_fusion
  185.7 20.5 %while.47 = (s32[]{:T(128)}, f32[4,256]{1,0:T(4,128)S(1)}, f32[4,256]{1,0:T(4,128)S(1)}, f32[4,256,128]{2,1,0:T(8,128)S(1)}, s32[8]{0:T(128)S(1)}, /*index=5*/s3...) while((s32[]{:T(128)}, f32[4,256]{1,0:T(4,128)S(1)}, ...), condition=%wide.region_10.11_spmd.clone, body=%wide.region_5.10_spmd.clone.sunk | while | flops 275909376 | bytes 11353485 | solution.py:240
  201.2 4.9 conditional.31
  209.9 5.9 %collective-permute-start.10 = (bf16[256,512]{0,1:T(8,128)(2,1)}, bf16[256,512]{0,1:T(8,128)(2,1)S(1)}, u32[]{:S(2)}, u32[]{:S(2)}) collective-permute-start(bf16[256,512]{0,1:T(8,128)(2,1)} %copy.716), channel_id=1, source_target_pairs={{24,0},{32,8},{40,16},{48,24},{56,32},{64,40},{72,48},{80,56},{88,... | collective-permute-start | bytes 786440 | tf_op jit(solution)/shard_map/ppermute | solution.py:28
  216.9 12.0 %collective-permute-start.9 = (bf16[256,512]{0,1:T(8,128)(2,1)}, bf16[256,512]{0,1:T(8,128)(2,1)}, u32[]{:S(2)}, u32[]{:S(2)}) collective-permute-start(bf16[256,512]{0,1:T(8,128)(2,1)} %copy.720), channel_id=1, source_target_pairs={{32,0},{40,8},{48,16},{56,24},{64,32},{72,40},{80,48},{88,56},{96,... | collective-permute-start | bytes 786440 | tf_op jit(solution)/shard_map/ppermute | solution.py:28
  234.9 25.1 %collective-permute-start.5 = (bf16[256,512]{0,1:T(8,128)(2,1)}, bf16[256,512]{0,1:T(8,128)(2,1)}, u32[]{:S(2)}, u32[]{:S(2)}) collective-permute-start(bf16[256,512]{0,1:T(8,128)(2,1)} %copy.720), channel_id=1, source_target_pairs={{48,0},{56,8},{64,16},{72,24},{80,32},{88,40},{96,48},{104,56},{11... | collective-permute-start | bytes 786440 | tf_op jit(solution)/shard_map/ppermute | solution.py:28
  261.4 27.9 %while.48 = (s32[]{:T(128)}, f32[256,4,128]{0,2,1:T(8,128)}, s32[8]{0:T(128)}, s32[]{:T(128)}, s32[]{:T(128)}, /*index=5*/bf16[4096,512]{0,1:T(8,128)(2,1)}, s32...) while((s32[]{:T(128)}, f32[256,4,128]{0,2,1:T(8,128)}, ...), condition=%wide.region_15.16_spmd.clone, body=%wide.region_12.15_spmd.clone.sunk | while | flops 406979328 | bytes 9739665 | solution.py:285
  282.1 7.2 %conditional.32 = (f32[256,4,128]{0,2,1:T(8,128)}) conditional(s32[]{:T(128)} %convert_element_type.432, (s32[]{:T(128)}, bf16[4096,512]{0,1:T(8,128)(2,1)}, s32[]{:T(128)}, s32[4096]{0:T(1024)}, s32[256]{0:T(256)S(1)}, /*index=5*/bf16[256,4,128]{2,0,1:T(8,128)(2,1)S(1)}, f32[4,256]{1,0:T(4,128)}, bf16[4096,512]{0,1:T(8,128)(2,1)}, ...), branch_computations={%region_13.13_spmd, %region_14.14_spmd} | conditional | flops 406979328 | bytes 9738326 | solution.py:283
  283.1 2.5 constant_dynamic-slice_fusion.2
  286.1 3.2 fusion.23
  294.5 31.2 %collective-permute-start.4 = (bf16[256,512]{0,1:T(8,128)(2,1)}, bf16[256,512]{0,1:T(8,128)(2,1)}, u32[]{:S(2)}, u32[]{:S(2)}) collective-permute-start(bf16[256,512]{0,1:T(8,128)(2,1)} %copy.716), channel_id=1, source_target_pairs={{48,0},{56,8},{64,16},{72,24},{80,32},{88,40},{96,48},{104,56},{11... | collective-permute-start | bytes 786440 | tf_op jit(solution)/shard_map/ppermute | solution.py:28
  335.8 46.9 %all_gather.51 = f32[4,4096]{0,1:T(8,128)S(1)} all-gather(f32[4,256]{0,1:T(8,128)S(1)} %bitcast.375), channel_id=1, replica_groups=mesh['dp'=4,'seq'=16,'head'=8] {'seq'}, dimensions={1}, use_global_device_ids=true | all-gather | bytes 69632 | tf_op jit(solution)/shard_map/all_gather | solution.py:246
  382.7 20.0 %all_gather.50 = f32[4,4096]{1,0:T(4,128)} all-gather(f32[4,256]{1,0:T(4,128)S(1)} %copy-done.30), channel_id=1, replica_groups=mesh['dp'=4,'seq'=16,'head'=8] {'seq'}, dimensions={1}, use_global_device_ids=true | all-gather | bytes 69632 | tf_op jit(solution)/shard_map/all_gather | solution.py:245
  403.7 9.7 %conditional.18 = (f32[256,4,128]{2,0,1:T(8,128)S(1)}, f32[256,4,128]{2,0,1:T(8,128)S(1)}) conditional(s32[]{:T(128)} %convert_element_type.269, (s32[256]{0:T(256)S(1)}, s32[]{:T(128)}, s32[256]{0:T(256)S(1)}, s32[4096]{0:T(1024)}, bf16[256,4,128]{0,2,1:T(8,128)(2,1)}, /*index=5*/bf16[256,4,128]{0,2,1:T(8,128)(2,1)S(1)}, f32[4,4096]{1,0:T(4,128)}, ...), branch_computations={%region_17.18_spmd, %region_18.19_spmd} | conditional | flops 271122688 | bytes 10255450 | solution.py:334
  406.0 2.4 fusion.37
  409.4 2.1 fusion.42
  413.4 8.6 %conditional.19 = ((f32[256,4,128]{2,0,1:T(8,128)S(1)}, f32[256,4,128]{2,0,1:T(8,128)S(1)})) conditional(s32[]{:T(128)} %convert_element_type.268, (s32[256]{0:T(256)S(1)}, s32[]{:T(128)}, s32[256]{0:T(256)S(1)}, s32[4096]{0:T(1024)}, bf16[256,4,128]{0,2,1:T(8,128)(2,1)}, /*index=5*/bf16[256,4,128]{0,2,1:T(8,128)(2,1)}, f32[4,4096]{1,0:T(4,128)}, ...), branch_computations={%region_19.20_spmd, %region_20.21_spmd} | conditional | flops 271122688 | bytes 7109702 | solution.py:334
  415.7 2.5 fusion.50
  418.2 2.1 fusion.55
  422.0 8.6 %conditional.20 = ((f32[256,4,128]{2,0,1:T(8,128)S(1)}, f32[256,4,128]{2,0,1:T(8,128)S(1)})) conditional(s32[]{:T(128)} %convert_element_type.267, (s32[256]{0:T(256)S(1)}, s32[]{:T(128)}, s32[256]{0:T(256)S(1)}, s32[4096]{0:T(1024)}, bf16[256,4,128]{0,2,1:T(8,128)(2,1)}, /*index=5*/bf16[256,4,128]{0,2,1:T(8,128)(2,1)}, f32[4,4096]{1,0:T(4,128)}, ...), branch_computations={%region_21.22_spmd, %region_22.23_spmd} | conditional | flops 271122688 | bytes 7109702 | solution.py:334
  424.3 2.5 fusion.63
  426.8 2.1 fusion.68
  430.6 8.8 %conditional.21 = ((f32[256,4,128]{2,0,1:T(8,128)S(1)}, f32[256,4,128]{2,0,1:T(8,128)S(1)})) conditional(s32[]{:T(128)} %convert_element_type.266, (s32[256]{0:T(256)S(1)}, s32[]{:T(128)}, s32[256]{0:T(256)S(1)}, s32[4096]{0:T(1024)}, bf16[256,4,128]{0,2,1:T(8,128)(2,1)}, /*index=5*/bf16[256,4,128]{0,2,1:T(8,128)(2,1)}, f32[4,4096]{1,0:T(4,128)}, ...), branch_computations={%region_23.24_spmd, %region_24.25_spmd} | conditional | flops 271122688 | bytes 7109702 | solution.py:334
  433.2 2.5 fusion.76
  435.7 2.1 fusion.81
  439.5 8.6 %conditional.22 = ((f32[256,4,128]{2,0,1:T(8,128)S(1)}, f32[256,4,128]{2,0,1:T(8,128)S(1)})) conditional(s32[]{:T(128)} %convert_element_type.265, (s32[256]{0:T(256)S(1)}, s32[]{:T(128)}, s32[256]{0:T(256)S(1)}, s32[4096]{0:T(1024)}, bf16[256,4,128]{0,2,1:T(8,128)(2,1)}, /*index=5*/bf16[256,4,128]{0,2,1:T(8,128)(2,1)}, f32[4,4096]{1,0:T(4,128)}, ...), branch_computations={%region_25.26_spmd, %region_26.27_spmd} | conditional | flops 271122688 | bytes 7109702 | solution.py:334
  441.8 2.5 fusion.89
  444.3 2.1 fusion.94
  448.1 8.6 %conditional.23 = ((f32[256,4,128]{2,0,1:T(8,128)S(1)}, f32[256,4,128]{2,0,1:T(8,128)S(1)})) conditional(s32[]{:T(128)} %convert_element_type.264, (s32[256]{0:T(256)S(1)}, s32[]{:T(128)}, s32[256]{0:T(256)S(1)}, s32[4096]{0:T(1024)}, bf16[256,4,128]{0,2,1:T(8,128)(2,1)}, /*index=5*/bf16[256,4,128]{0,2,1:T(8,128)(2,1)}, f32[4,4096]{1,0:T(4,128)}, ...), branch_computations={%region_27.28_spmd, %region_28.29_spmd} | conditional | flops 271122688 | bytes 7109702 | solution.py:334
  450.4 2.5 fusion.102
  452.9 2.1 fusion.107
  456.7 8.6 %conditional.24 = ((f32[256,4,128]{2,0,1:T(8,128)S(1)}, f32[256,4,128]{2,0,1:T(8,128)S(1)})) conditional(s32[]{:T(128)} %convert_element_type.263, (s32[256]{0:T(256)S(1)}, s32[]{:T(128)}, s32[256]{0:T(256)S(1)}, s32[4096]{0:T(1024)}, bf16[256,4,128]{0,2,1:T(8,128)(2,1)}, /*index=5*/bf16[256,4,128]{0,2,1:T(8,128)(2,1)}, f32[4,4096]{1,0:T(4,128)}, ...), branch_computations={%region_29.30_spmd, %region_30.31_spmd} | conditional | flops 271122688 | bytes 7109702 | solution.py:334
  459.0 2.5 fusion.115
  461.6 2.1 fusion.120
  465.4 8.6 %conditional.25 = ((f32[256,4,128]{2,0,1:T(8,128)S(1)}, f32[256,4,128]{2,0,1:T(8,128)S(1)})) conditional(s32[]{:T(128)} %convert_element_type.262, (s32[256]{0:T(256)S(1)}, s32[]{:T(128)}, s32[256]{0:T(256)S(1)}, s32[4096]{0:T(1024)}, bf16[256,4,128]{0,2,1:T(8,128)(2,1)}, /*index=5*/bf16[256,4,128]{0,2,1:T(8,128)(2,1)}, f32[4,4096]{1,0:T(4,128)}, ...), branch_computations={%region_31.32_spmd, %region_32.33_spmd} | conditional | flops 271122688 | bytes 7109702 | solution.py:334
  467.7 2.5 fusion.128
  470.2 2.1 fusion.133
  474.1 7.6 %conditional.26 = (bf16[256,512]{1,0:T(8,128)(2,1)S(1)}, bf16[256,512]{1,0:T(8,128)(2,1)S(1)}) conditional(s32[]{:T(128)} %convert_element_type.261, (s32[256]{0:T(256)S(1)}, s32[]{:T(128)}, s32[256]{0:T(256)S(1)}, s32[4096]{0:T(1024)}, bf16[256,512]{0,1:T(8,128)(2,1)}, /*index=5*/bf16[256,4,128]{0,2,1:T(8,128)(2,1)}, f32[4,4096]{1,0:T(4,128)}, ...), branch_computations={%region_33.34_spmd, %region_34.35_spmd} | conditional | flops 271384832 | bytes 10779738
  482.5 92.8 %while.45 = (s32[]{:T(128)}, f32[4,128,128]{2,1,0:T(8,128)S(1)}, f32[]{:T(128)}, s32[]{:T(128)}, f32[16]{0:T(128)S(1)}, /*index=5*/f32[16]{0:T(128)S(1)}, f32[16...) while((s32[]{:T(128)}, f32[4,128,128]{2,1,0:T(8,128)S(1)}, ...), condition=%wide.region_1.2_spmd, body=%wide.region_0.1_spmd.sunk | while | flops 262154 | bytes 786708 | solution.py:22
  (377 shorter events, 161.1 us)
Async XLA Ops:
  7.2 53.5 %copy-start = (bf16[256,512]{1,0:T(8,128)(2,1)S(1)}, bf16[256,512]{1,0:T(8,128)(2,1)}, u32[]{:S(2)}) copy-start(bf16[256,512]{1,0:T(8,128)(2,1)} %param.43) | copy-start | bytes 786436
  7.2 12.1 %copy-start.32 = (f32[4]{0:T(128)S(1)}, f32[4]{0:T(128)}, u32[]{:S(2)}) copy-start(f32[4]{0:T(128)} %param.44) | copy-start | bytes 52
  7.2 8.8 %copy-start.22 = (bf16[256,512]{1,0:T(8,128)(2,1)S(1)}, bf16[256,512]{1,0:T(8,128)(2,1)}, u32[]{:S(2)}) copy-start(bf16[256,512]{1,0:T(8,128)(2,1)} %param.48) | copy-start | bytes 786436
  7.2 9.8 %copy-start.23 = (bf16[256,512]{1,0:T(8,128)(2,1)S(1)}, bf16[256,512]{1,0:T(8,128)(2,1)}, u32[]{:S(2)}) copy-start(bf16[256,512]{1,0:T(8,128)(2,1)} %param.47) | copy-start | bytes 786436
  7.2 35.9 %copy-start.12 = (bf16[256,512]{1,0:T(8,128)(2,1)S(1)}, bf16[256,512]{1,0:T(8,128)(2,1)}, u32[]{:S(2)}) copy-start(bf16[256,512]{1,0:T(8,128)(2,1)} %param.42) | copy-start | bytes 786436
  7.2 52.0 %all-gather.14.cloned.1.call-start = ((), (), s32[]{:S(2)}) async-start(), calls=%async_computation.4 | async-start | bytes 4456448 | tf_op jit(solution)/shard_map/all_gather | solution.py:13
  7.3 35.9 %copy-start.34 = (f32[256]{0:T(256)}, f32[256]{0:T(256)S(1)}, u32[]{:S(2)}) copy-start(f32[256]{0:T(256)S(1)} %convert_negate_fusion) | copy-start | bytes 3076
  13.0 202.8 %copy-start.7 = (bf16[256,512]{0,1:T(8,128)(2,1)}, bf16[256,512]{0,1:T(8,128)(2,1)S(1)}, u32[]{:S(2)}) copy-start(bf16[256,512]{0,1:T(8,128)(2,1)S(1)} %copy.872) | copy-start | bytes 786436
  14.2 152.9 %copy-start.9 = (bf16[256,512]{0,1:T(8,128)(2,1)}, bf16[256,512]{0,1:T(8,128)(2,1)S(1)}, u32[]{:S(2)}) copy-start(bf16[256,512]{0,1:T(8,128)(2,1)S(1)} %copy.873) | copy-start | bytes 786436
  16.0 169.6 %all-gather.10.cloned.1.call-start = ((), (), s32[]{:S(2)}) async-start(), calls=%async_computation.2 | async-start | bytes 4456448 | tf_op jit(solution)/shard_map/all_gather | solution.py:179
  16.9 168.7 %all-gather.8.cloned.1.call-start = ((), (), s32[]{:S(2)}) async-start(), calls=%async_computation.1 | async-start | bytes 4456448 | tf_op jit(solution)/shard_map/all_gather | solution.py:178
  17.8 463.9 %all-gather.12.cloned.1.call-start = ((), (), s32[]{:S(2)}) async-start(), calls=%async_computation.3 | async-start | bytes 4456448 | tf_op jit(solution)/shard_map/all_gather | solution.py:13
  43.2 17.5 %copy-start.13 = (bf16[256,512]{0,1:T(8,128)(2,1)}, bf16[256,512]{0,1:T(8,128)(2,1)S(1)}, u32[]{:S(2)}) copy-start(bf16[256,512]{0,1:T(8,128)(2,1)S(1)} %copy.902) | copy-start | bytes 786436
  59.3 24.6 %copy-start.25 = (bf16[256,512]{1,0:T(8,128)(2,1)S(1)}, bf16[256,512]{1,0:T(8,128)(2,1)}, u32[]{:S(2)}) copy-start(bf16[256,512]{1,0:T(8,128)(2,1)} %param.46) | copy-start | bytes 786436
  59.4 107.7 %copy-start.31 = (f32[16,4]{1,0:T(8,128)}, f32[16,4]{1,0:T(8,128)S(1)}, u32[]{:S(2)}) copy-start(f32[16,4]{1,0:T(8,128)S(1)} %get-tuple-element.3290) | copy-start | bytes 772
  59.4 108.1 %copy-start.38 = (f32[16]{0:T(128)}, f32[16]{0:T(128)S(1)}, u32[]{:S(2)}) copy-start(f32[16]{0:T(128)S(1)} %get-tuple-element.3292) | copy-start | bytes 196
  62.6 147.3 %collective-permute-start.15 = (bf16[256,512]{0,1:T(8,128)(2,1)}, bf16[256,512]{0,1:T(8,128)(2,1)}, u32[]{:S(2)}, u32[]{:S(2)}) collective-permute-start(bf16[256,512]{0,1:T(8,128)(2,1)} %copy.720), channel_id=1, source_target_pairs={{8,0},{16,8},{24,16},{32,24},{40,32},{48,40},{56,48},{64,56},{72,6... | collective-permute-start | bytes 786440 | tf_op jit(solution)/shard_map/ppermute | solution.py:28
  71.0 157.9 %collective-permute-start.13 = (bf16[256,512]{0,1:T(8,128)(2,1)}, bf16[256,512]{0,1:T(8,128)(2,1)}, u32[]{:S(2)}, u32[]{:S(2)}) collective-permute-start(bf16[256,512]{0,1:T(8,128)(2,1)} %copy.720), channel_id=1, source_target_pairs={{16,0},{24,8},{32,16},{40,24},{48,32},{56,40},{64,48},{72,56},{80,... | collective-permute-start | bytes 786440 | tf_op jit(solution)/shard_map/ppermute | solution.py:28
  84.8 132.1 %collective-permute-start.14 = (bf16[256,512]{0,1:T(8,128)(2,1)}, bf16[256,512]{0,1:T(8,128)(2,1)}, u32[]{:S(2)}, u32[]{:S(2)}) collective-permute-start(bf16[256,512]{0,1:T(8,128)(2,1)} %copy.716), channel_id=1, source_target_pairs={{8,0},{16,8},{24,16},{32,24},{40,32},{48,40},{56,48},{64,56},{72,6... | collective-permute-start | bytes 786440 | tf_op jit(solution)/shard_map/ppermute | solution.py:28
  94.1 136.7 %collective-permute-start.12 = (bf16[256,512]{0,1:T(8,128)(2,1)}, bf16[256,512]{0,1:T(8,128)(2,1)}, u32[]{:S(2)}, u32[]{:S(2)}) collective-permute-start(bf16[256,512]{0,1:T(8,128)(2,1)} %copy.716), channel_id=1, source_target_pairs={{16,0},{24,8},{32,16},{40,24},{48,32},{56,40},{64,48},{72,56},{80,... | collective-permute-start | bytes 786440 | tf_op jit(solution)/shard_map/ppermute | solution.py:28
  107.5 125.4 %collective-permute-start.11 = (bf16[256,512]{0,1:T(8,128)(2,1)}, bf16[256,512]{0,1:T(8,128)(2,1)S(1)}, u32[]{:S(2)}, u32[]{:S(2)}) collective-permute-start(bf16[256,512]{0,1:T(8,128)(2,1)} %copy.720), channel_id=1, source_target_pairs={{24,0},{32,8},{40,16},{48,24},{56,32},{64,40},{72,48},{80,56},{88,... | collective-permute-start | bytes 786440 | tf_op jit(solution)/shard_map/ppermute | solution.py:28
  127.7 54.4 %all-to-all-start = ((s32[16,1,256]{2,1,0:T(1,128)}), s32[16,1,256]{2,1,0:T(1,128)}, u32[]{:S(2)}, u32[]{:S(2)}) async-start(s32[16,1,256]{2,1,0:T(1,128)} %stack.2), calls=%async_computation | async-start | bytes 32768 | tf_op jit(solution)/shard_map/all_to_all | solution.py:89
  167.5 48.4 %copy-start.5 = (f32[4,256,256]{2,1,0:T(8,128)}, f32[4,256,256]{2,1,0:T(8,128)S(1)}, u32[]{:S(2)}) copy-start(f32[4,256,256]{2,1,0:T(8,128)S(1)} %convolution_multiply_fusion.9) | copy-start | bytes 3145732
  208.9 52.5 %copy-start.16 = (f32[256,4]{1,0:T(8,128)}, f32[256,4]{1,0:T(8,128)S(1)}, u32[]{:S(2)}) copy-start(f32[256,4]{1,0:T(8,128)S(1)} %copy.870) | copy-start | bytes 12292
  209.9 25.0 %collective-permute-start.10 = (bf16[256,512]{0,1:T(8,128)(2,1)}, bf16[256,512]{0,1:T(8,128)(2,1)S(1)}, u32[]{:S(2)}, u32[]{:S(2)}) collective-permute-start(bf16[256,512]{0,1:T(8,128)(2,1)} %copy.716), channel_id=1, source_target_pairs={{24,0},{32,8},{40,16},{48,24},{56,32},{64,40},{72,48},{80,56},{88,... | collective-permute-start | bytes 786440 | tf_op jit(solution)/shard_map/ppermute | solution.py:28
  216.9 77.6 %collective-permute-start.9 = (bf16[256,512]{0,1:T(8,128)(2,1)}, bf16[256,512]{0,1:T(8,128)(2,1)}, u32[]{:S(2)}, u32[]{:S(2)}) collective-permute-start(bf16[256,512]{0,1:T(8,128)(2,1)} %copy.720), channel_id=1, source_target_pairs={{32,0},{40,8},{48,16},{56,24},{64,32},{72,40},{80,48},{88,56},{96,... | collective-permute-start | bytes 786440 | tf_op jit(solution)/shard_map/ppermute | solution.py:28
  228.9 96.9 %collective-permute-start.8 = (bf16[256,512]{0,1:T(8,128)(2,1)}, bf16[256,512]{0,1:T(8,128)(2,1)}, u32[]{:S(2)}, u32[]{:S(2)}) collective-permute-start(bf16[256,512]{0,1:T(8,128)(2,1)} %copy.716), channel_id=1, source_target_pairs={{32,0},{40,8},{48,16},{56,24},{64,32},{72,40},{80,48},{88,56},{96,... | collective-permute-start | bytes 786440 | tf_op jit(solution)/shard_map/ppermute | solution.py:28
  230.9 96.9 %collective-permute-start.7 = (bf16[256,512]{0,1:T(8,128)(2,1)}, bf16[256,512]{0,1:T(8,128)(2,1)}, u32[]{:S(2)}, u32[]{:S(2)}) collective-permute-start(bf16[256,512]{0,1:T(8,128)(2,1)} %copy.720), channel_id=1, source_target_pairs={{40,0},{48,8},{56,16},{64,24},{72,32},{80,40},{88,48},{96,56},{104... | collective-permute-start | bytes 786440 | tf_op jit(solution)/shard_map/ppermute | solution.py:28
  232.9 28.5 %copy-start.20 = (bf16[256,512]{0,1:T(8,128)(2,1)}, bf16[256,512]{0,1:T(8,128)(2,1)S(1)}, u32[]{:S(2)}) copy-start(bf16[256,512]{0,1:T(8,128)(2,1)S(1)} %collective-permute-done.11) | copy-start | bytes 786436
  232.9 96.8 %collective-permute-start.6 = (bf16[256,512]{0,1:T(8,128)(2,1)}, bf16[256,512]{0,1:T(8,128)(2,1)}, u32[]{:S(2)}, u32[]{:S(2)}) collective-permute-start(bf16[256,512]{0,1:T(8,128)(2,1)} %copy.716), channel_id=1, source_target_pairs={{40,0},{48,8},{56,16},{64,24},{72,32},{80,40},{88,48},{96,56},{104... | collective-permute-start | bytes 786440 | tf_op jit(solution)/shard_map/ppermute | solution.py:28
  234.9 26.5 %copy-start.28 = (bf16[256,512]{0,1:T(8,128)(2,1)}, bf16[256,512]{0,1:T(8,128)(2,1)S(1)}, u32[]{:S(2)}) copy-start(bf16[256,512]{0,1:T(8,128)(2,1)S(1)} %collective-permute-done.10) | copy-start | bytes 786436
  234.9 96.9 %collective-permute-start.5 = (bf16[256,512]{0,1:T(8,128)(2,1)}, bf16[256,512]{0,1:T(8,128)(2,1)}, u32[]{:S(2)}, u32[]{:S(2)}) collective-permute-start(bf16[256,512]{0,1:T(8,128)(2,1)} %copy.720), channel_id=1, source_target_pairs={{48,0},{56,8},{64,16},{72,24},{80,32},{88,40},{96,48},{104,56},{11... | collective-permute-start | bytes 786440 | tf_op jit(solution)/shard_map/ppermute | solution.py:28
  289.3 44.4 %copy-start.3 = (f32[4,256,256]{2,1,0:T(8,128)S(1)}, f32[4,256,256]{2,1,0:T(8,128)}, u32[]{:S(2)}) copy-start(f32[4,256,256]{2,1,0:T(8,128)} %convolution_multiply_fusion.10) | copy-start | bytes 3145732
  289.3 44.4 %copy-start.10 = (bf16[256,512]{0,1:T(8,128)(2,1)S(1)}, bf16[256,512]{0,1:T(8,128)(2,1)}, u32[]{:S(2)}) copy-start(bf16[256,512]{0,1:T(8,128)(2,1)} %copy-done.9) | copy-start | bytes 786436
  291.3 43.6 %copy-start.19 = (bf16[4,256,128]{1,2,0:T(8,128)(2,1)S(1)}, bf16[4,256,128]{1,2,0:T(8,128)(2,1)}, u32[]{:S(2)}) copy-start(bf16[4,256,128]{1,2,0:T(8,128)(2,1)} %get-tuple-element.2722) | copy-start | bytes 786436
  293.2 42.7 %copy-start.17 = (f32[256,4]{1,0:T(8,128)S(1)}, f32[256,4]{1,0:T(8,128)}, u32[]{:S(2)}) copy-start(f32[256,4]{1,0:T(8,128)} %copy-done.16) | copy-start | bytes 12292
  294.5 162.2 %collective-permute-start.4 = (bf16[256,512]{0,1:T(8,128)(2,1)}, bf16[256,512]{0,1:T(8,128)(2,1)}, u32[]{:S(2)}, u32[]{:S(2)}) collective-permute-start(bf16[256,512]{0,1:T(8,128)(2,1)} %copy.716), channel_id=1, source_target_pairs={{48,0},{56,8},{64,16},{72,24},{80,32},{88,40},{96,48},{104,56},{11... | collective-permute-start | bytes 786440 | tf_op jit(solution)/shard_map/ppermute | solution.py:28
  325.8 139.6 %collective-permute-start.3 = (bf16[256,512]{0,1:T(8,128)(2,1)}, bf16[256,512]{0,1:T(8,128)(2,1)}, u32[]{:S(2)}, u32[]{:S(2)}) collective-permute-start(bf16[256,512]{0,1:T(8,128)(2,1)} %copy.720), channel_id=1, source_target_pairs={{56,0},{64,8},{72,16},{80,24},{88,32},{96,40},{104,48},{112,56},{1... | collective-permute-start | bytes 786440 | tf_op jit(solution)/shard_map/ppermute | solution.py:28
  327.7 137.6 %collective-permute-start.2 = (bf16[256,512]{0,1:T(8,128)(2,1)}, bf16[256,512]{0,1:T(8,128)(2,1)}, u32[]{:S(2)}, u32[]{:S(2)}) collective-permute-start(bf16[256,512]{0,1:T(8,128)(2,1)} %copy.716), channel_id=1, source_target_pairs={{56,0},{64,8},{72,16},{80,24},{88,32},{96,40},{104,48},{112,56},{1... | collective-permute-start | bytes 786440 | tf_op jit(solution)/shard_map/ppermute | solution.py:28
  329.7 144.3 %collective-permute-start.1 = (bf16[256,512]{0,1:T(8,128)(2,1)}, bf16[256,512]{0,1:T(8,128)(2,1)}, u32[]{:S(2)}, u32[]{:S(2)}) collective-permute-start(bf16[256,512]{0,1:T(8,128)(2,1)} %copy.720), channel_id=1, source_target_pairs={{64,0},{72,8},{80,16},{88,24},{96,32},{104,40},{112,48},{120,56},{... | collective-permute-start | bytes 786440 | tf_op jit(solution)/shard_map/ppermute | solution.py:28
  331.7 142.3 %collective-permute-start = (bf16[256,512]{0,1:T(8,128)(2,1)}, bf16[256,512]{0,1:T(8,128)(2,1)}, u32[]{:S(2)}, u32[]{:S(2)}) collective-permute-start(bf16[256,512]{0,1:T(8,128)(2,1)} %copy.716), channel_id=1, source_target_pairs={{64,0},{72,8},{80,16},{88,24},{96,32},{104,40},{112,48},{120,56},{... | collective-permute-start | bytes 786440 | tf_op jit(solution)/shard_map/ppermute | solution.py:28
  334.1 48.7 %copy-start.30 = (f32[4,256]{1,0:T(4,128)S(1)}, f32[4,256]{1,0:T(4,128)}, u32[]{:S(2)}) copy-start(f32[4,256]{1,0:T(4,128)} %get-tuple-element.3289) | copy-start | bytes 12292
  334.1 69.5 %copy-start.1 = (bf16[256,512]{0,1:T(8,128)(2,1)S(1)}, bf16[256,512]{0,1:T(8,128)(2,1)}, u32[]{:S(2)}) copy-start(bf16[256,512]{0,1:T(8,128)(2,1)} %copy.717) | copy-start | bytes 786436
  334.1 69.5 %copy-start.18 = (bf16[256,512]{0,1:T(8,128)(2,1)S(1)}, bf16[256,512]{0,1:T(8,128)(2,1)}, u32[]{:S(2)}) copy-start(bf16[256,512]{0,1:T(8,128)(2,1)} %copy.715) | copy-start | bytes 786436
  481.8 93.6 %copy-start.33 = (f32[4]{0:T(128)S(1)}, f32[4]{0:T(128)}, u32[]{:S(2)}) copy-start(f32[4]{0:T(128)} %param.44) | copy-start | bytes 52
  481.8 93.6 %copy-start.35 = (f32[256]{0:T(256)S(1)}, f32[256]{0:T(256)}, u32[]{:S(2)}) copy-start(f32[256]{0:T(256)} %copy-done.34) | copy-start | bytes 3076
  481.8 93.6 %copy-start.11 = (bf16[256,512]{0,1:T(8,128)(2,1)S(1)}, bf16[256,512]{0,1:T(8,128)(2,1)}, u32[]{:S(2)}) copy-start(bf16[256,512]{0,1:T(8,128)(2,1)} %copy-done.9) | copy-start | bytes 786436
  481.8 94.0 %copy-start.8 = (bf16[256,512]{0,1:T(8,128)(2,1)S(1)}, bf16[256,512]{0,1:T(8,128)(2,1)}, u32[]{:S(2)}) copy-start(bf16[256,512]{0,1:T(8,128)(2,1)} %copy-done.7) | copy-start | bytes 786436
  (13 other events, 34.5 us)
Sparse Core Ops, SparseCore 0:
  16.1 43.1 all-gather.13
  61.3 50.4 all-gather.9
  114.4 61.3 all-gather.7
  178.4 46.6 all-gather.11
